TPU v7x, 256 devices: a whole 4x4x8 slice. The times are simulated.
256 devices in a mesh: segment: 4 (over y), ctx: 32 (over x_hi, z, core), tp: 2 (over x_lo).
Axes of the slice: x: 4 (x_hi: 2, x_lo: 2; x = x_hi * 2 + x_lo), y: 4, z: 8, core: 2. Of those that a mesh axis runs over, the one named last changes fastest.
Arguments:
- held: bfloat16 [4, 8192, 3584], P('segment', 'ctx'), may hold values from -6 to 6
- text: bfloat16 [8192, 3584], P('ctx'), may hold values from -6 to 6
- frames: bfloat16 [4096, 1024], P('ctx'), may hold values from -6 to 6
- join: int32 [64], P('ctx'), may hold values from 0 to 8128, as said below
- ln_gain: float32 [1024], replicated, may hold values from 0.1 to 1.9
- w_proj: bfloat16 [1024, 3584], P('tp'), may hold values from -0.1875 to 0.1875
- b_proj: float32 [3584], replicated, may hold values from -3 to 3
- norm_gain: float32 [3, 3584], replicated, may hold values from 0.1 to 1.9
- w_qkv: bfloat16 [3, 3584, 2304], P(None, 'ctx', 'tp'), may hold values from -0.09375 to 0.09375
- b_qkv: float32 [3, 2304], P(None, 'tp'), may hold values from -4 to 4
- w_out: bfloat16 [3, 1792, 3584], P(None, 'tp', 'ctx'), may hold values from -1.5 to 1.5
Outputs:
- segment_out: bfloat16 [4, 8192, 3584], P('segment', 'ctx')
Inputs may be any that keep to these rules, and one draw needn't show every extreme that they name: `join`: frames never intersect; the 2 frames f with f // 2 == d lie in order inside positions d * 256 to (d + 1) * 256 - 1.
All inputs are finite; a program needn't handle non-finite values.
Results may differ from a plain program's by a relative error of at most 0.015.
Values may be sent and summed in bfloat16 or wider, within the bound.
No kernel may reach another device: no remote copies, remote signals or barrier semaphores. Data moves between devices by JAX's collectives and lax.ppermute only.
A program may use at most 128 MiB of HBM per device.

v0:
```python
from functools import partial

import jax
import jax.numpy as jnp
from jax import lax
from jax.sharding import PartitionSpec as P

HD = 128
GROUP = 7
FRAME = 64


def shifted(value, axis, by):
    devices = lax.axis_size(axis)
    pairs = [(i, i + by) for i in range(devices) if 0 <= i + by < devices]
    return lax.ppermute(value, axis, pairs)


def update_state(softmax_state, query_flat, query_pos, keys_in, values_in, offset):
    peak_old, total_old, accum_old = softmax_state
    key_pos = jnp.arange(keys_in.shape[0], dtype=jnp.int32)
    scores = jnp.dot(query_flat, keys_in.T, preferred_element_type=jnp.float32) * HD ** (-0.5)
    allowed = key_pos[None, :] <= query_pos[:, None]
    scores = jnp.where(allowed, scores, -1e30)
    peak_new = jnp.maximum(peak_old, jnp.max(scores, axis=1))
    weights = jnp.where(allowed, jnp.exp(scores - peak_new[:, None]), 0.0)
    total_new = jnp.sum(weights, axis=1)
    accum_new = jnp.dot(weights.astype(jnp.bfloat16), values_in, preferred_element_type=jnp.float32)
    return (peak_new, total_new, accum_new)


def keep_state(softmax_state):
    return softmax_state


def on_device(held, text, frames, join, ln_gain, w_proj, b_proj, norm_gain, w_qkv, b_qkv, w_out):
    segment_id = lax.axis_index("segment")
    ctx_id = lax.axis_index("ctx")
    tp_id = lax.axis_index("tp")
    hidden_in = shifted(held[0], "segment", 1)
    tok_rows = hidden_in.shape[0]
    half_rows = tok_rows // 2
    layer_id = jnp.maximum(segment_id - 1, 0)
    weight_qkv = lax.dynamic_index_in_dim(w_qkv, layer_id, 0, keepdims=False)
    bias_qkv = lax.dynamic_index_in_dim(b_qkv, layer_id, 0, keepdims=False)
    layer_gain = lax.dynamic_index_in_dim(norm_gain, layer_id, 0, keepdims=False)
    weight_out = lax.dynamic_index_in_dim(w_out, layer_id, 0, keepdims=False)
    inputs = hidden_in.astype(jnp.float32)
    normed = (
        inputs * lax.rsqrt(jnp.mean(inputs * inputs, axis=1, keepdims=True) + 1e-06) * layer_gain
    ).astype(jnp.bfloat16)
    merged = jnp.dot(
        normed,
        lax.all_gather(weight_qkv, "ctx", axis=0, tiled=True),
        preferred_element_type=jnp.float32,
    )
    merged = (merged + bias_qkv).astype(jnp.bfloat16)
    query_cols = GROUP * HD
    queries = merged[:, :query_cols]
    key_part = merged[:, query_cols : query_cols + HD]
    value_part = merged[:, query_cols + HD : query_cols + 2 * HD]
    local_steps = jnp.arange(half_rows, dtype=jnp.int32)
    first_pos = ctx_id * tok_rows + local_steps
    second_q = queries[half_rows:]
    second_pos = ctx_id * tok_rows + half_rows + local_steps
    first_flat = queries[:half_rows].reshape(half_rows * GROUP, HD)
    second_flat = second_q.reshape(half_rows * GROUP, HD)
    first_qpos = jnp.repeat(first_pos, GROUP)
    second_qpos = jnp.repeat(second_pos, GROUP)
    flat_rows = half_rows * GROUP
    empty = (
        jnp.full((flat_rows,), -1e30, jnp.float32),
        jnp.zeros((flat_rows,), jnp.float32),
        jnp.zeros((flat_rows, HD), jnp.float32),
    )
    carried = (empty, empty)
    offset = jnp.int32(0)
    keys_in = lax.all_gather(key_part, "ctx", axis=0, tiled=True)
    values_in = lax.all_gather(value_part, "ctx", axis=0, tiled=True)
    updated = []
    for softmax_state, query_flat, query_pos in (
        (carried[0], first_flat, first_qpos),
        (carried[1], second_flat, second_qpos),
    ):
        step_fn = partial(
            update_state,
            query_flat=query_flat,
            query_pos=query_pos,
            keys_in=keys_in,
            values_in=values_in,
            offset=offset,
        )
        updated.append(lax.cond(offset <= jnp.max(query_pos), step_fn, keep_state, softmax_state))

    def finish(softmax_state):
        return (
            (softmax_state[2] / softmax_state[1][:, None])
            .astype(jnp.bfloat16)
            .reshape(half_rows, GROUP * HD)
        )

    first_out = finish(updated[0])
    second_out = finish(updated[1])
    attended = jnp.concatenate([first_out, second_out], axis=0)
    partial_model = jnp.dot(
        attended,
        lax.all_gather(weight_out, "ctx", axis=1, tiled=True),
        preferred_element_type=jnp.float32,
    )
    positions = ctx_id * tok_rows + jnp.arange(tok_rows, dtype=jnp.int32)[:, None]
    starts = join[None, :]
    inside = (positions >= starts) & (positions < starts + FRAME)
    frame_base = (jnp.arange(join.shape[0], dtype=jnp.int32) * FRAME)[None, :]
    source = jnp.sum(jnp.where(inside, frame_base + positions - starts, 0), axis=1)
    is_vision = jnp.any(inside, axis=1)

    def vision_term():
        frame_in = frames.astype(jnp.float32)
        center = jnp.mean(frame_in, axis=1, keepdims=True)
        spread = jnp.mean((frame_in - center) * (frame_in - center), axis=1, keepdims=True)
        normed_frames = ((frame_in - center) * lax.rsqrt(spread + 1e-06) * ln_gain).astype(
            jnp.bfloat16
        )
        vis_width = w_proj.shape[0]
        normed_half = lax.dynamic_slice_in_dim(normed_frames, tp_id * vis_width, vis_width, 1)
        projected = jnp.dot(normed_half, w_proj, preferred_element_type=jnp.float32)
        return jnp.where(is_vision[:, None], jnp.take(projected, source, axis=0), 0.0)

    def model_term():
        return partial_model

    is_first = segment_id == 0
    section_term = lax.cond(is_first, vision_term, model_term)
    baseline = jnp.where(
        is_first, jnp.where(is_vision[:, None], b_proj[None, :], text.astype(jnp.float32)), inputs
    )
    summed = lax.psum(section_term.astype(jnp.bfloat16), "tp").astype(jnp.float32)
    result = (baseline + summed).astype(jnp.bfloat16)
    return result[None]


def solution(mesh):
    return jax.shard_map(
        on_device,
        mesh=mesh,
        in_specs=(
            P("segment", "ctx", None),
            P("ctx", None),
            P("ctx", None),
            P("ctx"),
            P(),
            P("tp", None),
            P(),
            P(),
            P(None, "ctx", "tp"),
            P(None, "tp"),
            P(None, "tp", "ctx"),
        ),
        out_specs=P("segment", "ctx", None),
        check_vma=False,
    )
```

profile of v0, /device:TPU:230, one launch (start us, length us, event | category | flops | bytes accessed | tf_op | source)
XLA Modules:
  0.0 455.1 jit_solution(11434149428011326203)
XLA Ops:
  6.5 0.0 copy-start
  6.5 0.0 all-gather.11.cloned.1.call-start
  6.5 1.1 copy-done
  7.7 0.7 constant_dynamic-slice_fusion.1
  8.4 0.0 all-gather.11.cloned.1.call-update
  8.4 0.0 all-gather.7.cloned.1.call-start
  8.5 3.6 collective-permute-start
  12.1 0.7 dynamic-slice_reduce_fusion.1
  12.8 0.9 dynamic-slice_reduce_fusion
  13.7 37.8 %collective-permute-done = bf16[256,3584]{1,0:T(8,128)(2,1)S(1)} collective-permute-done((bf16[256,3584]{1,0:T(8,128)(2,1)}, bf16[256,3584]{1,0:T(8,128)(2,1)S(1)}, u32[]{:S(2)}, u32[]{:S(2)}) %collective-permute-start) | collective-permute-done | bytes 1835040 | tf_op jit(solution)/shard_map/ppermute | solution.py:16
  51.5 0.4 fusion.31
  52.0 0.0 copy-start.5
  52.0 56.5 %all-gather.11.cloned.1.call-done = bf16[1,3584,1152]{2,1,0:T(8,128)(2,1)} async-done(((bf16[1,112,1152]{2,1,0:T(8,128)(2,1)}), bf16[1,3584,1152]{2,1,0:T(8,128)(2,1)}) %all-gather.11.cloned.1.call-update) | async-done | bytes 8257552 | tf_op jit(solution)/shard_map/all_gather | solution.py:54
  108.5 5.9 %fusion.37 = bf16[256,1152]{1,0:T(8,128)(2,1)S(1)} fusion(bf16[1,3584,1152]{2,1,0:T(8,128)(2,1)} %all-gather.11.cloned.1.call-done, bf16[256,3584]{1,0:T(8,128)(2,1)S(1)} %collective-permute-done, f32[3584]{0:T(1024)S(1)} %dynamic-slice_reduce_fusion, f32[256]{0:T(256)S(1)} %add_rsqrt_fusion.1, f32[1152]{0:T(1024)S(1)} %dynamic-slice_reduce_fusion.1), kind=kOutput, calls=%fused_computation.56 | convolution fusion | flops 2118189056 | bytes 10702336 | tf_op jit(solution)/shard_map/dot_general | solution.py:52
  114.4 0.0 copy-done.2
  114.4 0.6 fusion.49
  115.1 0.0 all-gather.7.cloned.1.call-update
  115.1 0.0 all-gather.9.cloned.1.call-start
  115.1 0.7 all-gather.9.cloned.1.call-update
  115.8 0.0 all-gather.13.cloned.1.call-start
  115.9 1.6 constant_dynamic-slice_fusion
  117.5 0.0 all-gather.13.cloned.1.call-update
  117.5 0.0 all-reduce.2.cloned.1.call-start
  117.6 0.7 broadcast_reduce_fusion.1
  118.9 0.7 broadcast_reduce_fusion
  120.2 0.0 copy-done.5
  120.2 0.1 fusion.48
  120.3 0.1 ge.21
  120.4 71.1 %all-gather.7.cloned.1.call-done = bf16[8192,128]{1,0:T(8,128)(2,1)} async-done(((bf16[256,128]{1,0:T(8,128)(2,1)}), bf16[8192,128]{1,0:T(8,128)(2,1)}) %all-gather.7.cloned.1.call-update) | async-done | bytes 2097168 | tf_op jit(solution)/shard_map/all_gather | solution.py:78
  191.5 79.4 %all-gather.9.cloned.1.call-done = bf16[8192,128]{1,0:T(8,128)(2,1)} async-done(((bf16[256,128]{1,0:T(8,128)(2,1)}), bf16[8192,128]{1,0:T(8,128)(2,1)}) %all-gather.9.cloned.1.call-update) | async-done | bytes 2097168 | tf_op jit(solution)/shard_map/all_gather | solution.py:79
  270.9 0.1 broadcast_in_dim.104
  271.0 42.1 %conditional.3 = (f32[896]{0:T(1024)S(1)}, f32[896,128]{1,0:T(8,128)S(1)}) conditional(s32[]{:T(128)} %convert_element_type.51, () %tuple.27, (s32[128,7]{1,0:T(8,128)S(1)}, bf16[256,1152]{1,0:T(8,128)(2,1)S(1)}, bf16[8192,128]{1,0:T(8,128)(2,1)}, bf16[8192,128]{1,0:T(8,128)(2,1)}) %tuple.28), branch_computations={%region_3.4_spmd, %region_4.7_spmd} | conditional | flops 3875535872 | bytes 102308392 | solution.py:93
  271.0 0.2 le.30
  271.2 0.2 reshape.63
  271.5 14.0 %fusion = (f32[896]{0:T(1024)S(1)}, f32[896,8192]{1,0:T(8,128)}) fusion(s32[896]{0:T(1024)S(1)} %le.30, bf16[896,128]{1,0:T(8,128)(2,1)S(1)} %reshape.63, bf16[8192,128]{1,0:T(8,128)(2,1)} %get-tuple-element.43), kind=kOutput, calls=%fused_computation.4 | convolution fusion | flops 1908407424 | bytes 31693824 | tf_op jit(solution)/shard_map/cond/branch_1_fun/dot_general | solution.py:22
  285.5 13.1 %fusion.3 = f32[896,128]{1,0:T(8,128)S(1)} fusion(bf16[8192,128]{1,0:T(8,128)(2,1)S(1)} %copy-done.7, f32[896,8192]{1,0:T(8,128)} %get-tuple-element.86, f32[896]{0:T(1024)S(1)} %broadcast_maximum_fusion, s32[896]{0:T(1024)S(1)} %le.30), kind=kOutput, calls=%fused_computation.7 | convolution fusion | flops 1923088384 | bytes 31923200 | tf_op jit(solution)/shard_map/cond/branch_1_fun/dot_general | solution.py:28
  298.7 14.4 %fusion.2 = f32[896]{0:T(1024)S(1)} fusion(f32[896,8192]{1,0:T(8,128)} %get-tuple-element.86, f32[896]{0:T(1024)S(1)} %broadcast_maximum_fusion, s32[896]{0:T(1024)S(1)} %le.30), kind=kLoop, calls=%fused_computation.6 | loop fusion | flops 44039296 | bytes 29370880 | tf_op jit(solution)/shard_map/cond/branch_1_fun/reduce_sum | solution.py:27
  313.1 0.2 divide_convert_fusion.1
  313.3 0.2 reshape.67
  313.6 0.1 broadcast_in_dim.105
  313.7 0.0 copy-start.6
  313.7 42.8 %conditional.4 = (f32[896]{0:T(1024)S(1)}, f32[896,128]{1,0:T(8,128)S(1)}) conditional(s32[]{:T(128)} %convert_element_type.55, () %tuple.29, (s32[128,7]{1,0:T(8,128)S(1)}, bf16[256,1152]{1,0:T(8,128)(2,1)S(1)}, bf16[8192,128]{1,0:T(8,128)(2,1)}, bf16[8192,128]{1,0:T(8,128)(2,1)}) %tuple.30), branch_computations={%region_8.9_spmd, %region_9.12_spmd} | conditional | flops 3875535872 | bytes 102308392 | solution.py:93
  313.9 0.2 le.38
  314.1 0.2 reshape.64
  314.4 14.4 %fusion.8 = (f32[896]{0:T(1024)S(1)}, f32[896,8192]{1,0:T(8,128)}) fusion(s32[896]{0:T(1024)S(1)} %le.38, bf16[896,128]{1,0:T(8,128)(2,1)S(1)} %reshape.64, bf16[8192,128]{1,0:T(8,128)(2,1)} %get-tuple-element.47), kind=kOutput, calls=%fused_computation.15 | convolution fusion | flops 1908407424 | bytes 31693824 | tf_op jit(solution)/shard_map/cond/branch_1_fun/dot_general | solution.py:22
  328.8 0.0 copy-done.8
  328.8 13.0 %fusion.11 = f32[896,128]{1,0:T(8,128)S(1)} fusion(bf16[8192,128]{1,0:T(8,128)(2,1)S(1)} %copy-done.8, f32[896,8192]{1,0:T(8,128)} %get-tuple-element.88, f32[896]{0:T(1024)S(1)} %broadcast_maximum_fusion.1, s32[896]{0:T(1024)S(1)} %le.38), kind=kOutput, calls=%fused_computation.18 | convolution fusion | flops 1923088384 | bytes 31923200 | tf_op jit(solution)/shard_map/cond/branch_1_fun/dot_general | solution.py:28
  341.8 14.7 %fusion.10 = f32[896]{0:T(1024)S(1)} fusion(f32[896,8192]{1,0:T(8,128)} %get-tuple-element.88, f32[896]{0:T(1024)S(1)} %broadcast_maximum_fusion.1, s32[896]{0:T(1024)S(1)} %le.38), kind=kLoop, calls=%fused_computation.17 | loop fusion | flops 44039296 | bytes 29370880 | tf_op jit(solution)/shard_map/cond/branch_1_fun/reduce_sum | solution.py:27
  356.5 0.2 divide_convert_fusion
  356.7 0.2 reshape.68
  356.9 7.7 %all-gather.13.cloned.1.call-done = bf16[1,896,3584]{1,2,0:T(8,128)(2,1)} async-done(((bf16[1,896,112]{1,2,0:T(8,128)(2,1)}), bf16[1,896,3584]{1,2,0:T(8,128)(2,1)}) %all-gather.13.cloned.1.call-update) | async-done | bytes 6422544 | tf_op jit(solution)/shard_map/all_gather | solution.py:107
  364.6 0.0 copy-done.3
  364.6 6.2 %fusion.27 = bf16[256,3584]{1,0:T(8,128)(2,1)} fusion(bf16[1,896,3584]{1,2,0:T(8,128)(2,1)} %all-gather.13.cloned.1.call-done, bf16[128,896]{1,0:T(8,128)(2,1)S(1)} %reshape.68, bf16[128,896]{1,0:T(8,128)(2,1)S(1)} %reshape.67), kind=kOutput, calls=%fused_computation.45 | convolution fusion | flops 1645084672 | bytes 8716288 | tf_op jit(solution)/shard_map/dot_general | solution.py:105
  370.8 7.3 %conditional.5 = (bf16[256,3584]{1,0:T(8,128)(2,1)}) conditional(s32[]{:T(128)} %convert_element_type.50, bf16[256,3584]{1,0:T(8,128)(2,1)} %fusion.27, (pred[256]{0:T(512)(128)(4,1)S(1)}, pred[256,2]{0,1:T(4,128)(4,1)S(1)}, bf16[128,1024]{1,0:T(8,128)(2,1)S(1)}, f32[1024]{0:T(1024)S(1)}, s32[]{:T(128)}, /*index=5*/bf16[512,3584]{1,0:T(8,128)(2,1)}, ...), branch_computations={%region_13.14_spmd, %region_14.17_spmd} | conditional | flops 472585344 | bytes 13264226 | solution.py:133
  370.8 0.1 dynamic-slice
  370.9 0.1 convert_reduce_fusion
  371.0 0.2 multiply_reduce_fusion
  371.2 2.7 fusion.18
  374.0 0.1 fusion.23
  374.1 1.7 gather_fusion
  375.8 2.2 select_select_fusion
  378.1 0.0 all-reduce.2.cloned.1.call-update
  378.1 65.7 %all-reduce.2.cloned.1.call-done = bf16[256,3584]{1,0:T(8,128)(2,1)} async-done(((bf16[256,3584]{1,0:T(8,128)(2,1)}), bf16[256,3584]{1,0:T(8,128)(2,1)}) %all-reduce.2.cloned.1.call-update) | async-done | bytes 1835024 | tf_op jit(solution)/shard_map/psum | solution.py:137
  443.8 4.8 %fusion.41 = bf16[1,256,3584]{2,1,0:T(8,128)(2,1)} fusion(bf16[256,3584]{1,0:T(8,128)(2,1)} %all-reduce.2.cloned.1.call-done, bf16[256,3584]{1,0:T(8,128)(2,1)} %copy-done.2, bf16[256,3584]{1,0:T(8,128)(2,1)} %param.18, f32[3584]{0:T(1024)S(1)} %copy-done.4, pred[256]{0:T(512)(128)(4,1)S(1)} %get-tuple-element.83, pred[]{:T(512)S(6)} %eq.3), kind=kLoop, calls=%fused_computation.57 | loop fusion | flops 6422528 | bytes 7354625 | tf_op jit(solution)/shard_map/broadcast_in_dim | solution.py:139
  (27 shorter events, 0.1 us)
Async XLA Ops:
  6.5 1.1 copy-start
  6.5 101.9 %all-gather.11.cloned.1.call-start = ((), (), s32[]{:S(2)}) async-start(), calls=%async_computation.3 | async-start | bytes 8515584 | tf_op jit(solution)/shard_map/all_gather | solution.py:54
  8.4 183.1 %all-gather.7.cloned.1.call-start = ((), (), s32[]{:S(2)}) async-start(), calls=%async_computation | async-start | bytes 2162688 | tf_op jit(solution)/shard_map/all_gather | solution.py:78
  8.5 43.1 %collective-permute-start = (bf16[256,3584]{1,0:T(8,128)(2,1)}, bf16[256,3584]{1,0:T(8,128)(2,1)S(1)}, u32[]{:S(2)}, u32[]{:S(2)}) collective-permute-start(bf16[256,3584]{1,0:T(8,128)(2,1)} %bitcast.20), channel_id=1, source_target_pairs={{0,64},{64,128},{128,192},{1,65},{65,129},{129,193},{2,66},{66,130... | collective-permute-start | bytes 5505032 | tf_op jit(solution)/shard_map/ppermute | solution.py:16
  51.5 62.9 %copy-start.2 = (bf16[256,3584]{1,0:T(8,128)(2,1)}, bf16[256,3584]{1,0:T(8,128)(2,1)S(1)}, u32[]{:S(2)}) copy-start(bf16[256,3584]{1,0:T(8,128)(2,1)S(1)} %collective-permute-done) | copy-start | bytes 5505028
  52.0 68.2 %copy-start.5 = (s32[2]{0:T(128)S(1)}, s32[2]{0:T(128)}, u32[]{:S(2)}) copy-start(s32[2]{0:T(128)} %param.20) | copy-start | bytes 28
  115.1 155.8 %all-gather.9.cloned.1.call-start = ((), (), s32[]{:S(2)}) async-start(), calls=%async_computation.1 | async-start | bytes 2162688 | tf_op jit(solution)/shard_map/all_gather | solution.py:79
  115.8 248.8 %all-gather.13.cloned.1.call-start = ((), (), s32[]{:S(2)}) async-start(), calls=%async_computation.4 | async-start | bytes 6623232 | tf_op jit(solution)/shard_map/all_gather | solution.py:107
  117.5 326.3 %all-reduce.2.cloned.1.call-start = ((), (), s32[]{:S(2)}) async-start(), calls=%async_computation.2 | async-start | bytes 3670016 | tf_op jit(solution)/shard_map/psum | solution.py:137
  271.5 14.1 %copy-start.7 = (bf16[8192,128]{1,0:T(8,128)(2,1)S(1)}, bf16[8192,128]{1,0:T(8,128)(2,1)}, u32[]{:S(2)}) copy-start(bf16[8192,128]{1,0:T(8,128)(2,1)} %get-tuple-element.44) | copy-start | bytes 6291460 | tf_op jit(solution)/shard_map/cond
  313.7 51.0 %copy-start.3 = (bf16[128,1024]{1,0:T(8,128)(2,1)S(1)}, bf16[128,1024]{1,0:T(8,128)(2,1)}, u32[]{:S(2)}) copy-start(bf16[128,1024]{1,0:T(8,128)(2,1)} %param.19) | copy-start | bytes 786436
  313.7 51.0 %copy-start.6 = (f32[1024]{0:T(1024)S(1)}, f32[1024]{0:T(1024)}, u32[]{:S(2)}) copy-start(f32[1024]{0:T(1024)} %param.21) | copy-start | bytes 12292
  314.4 14.4 %copy-start.8 = (bf16[8192,128]{1,0:T(8,128)(2,1)S(1)}, bf16[8192,128]{1,0:T(8,128)(2,1)}, u32[]{:S(2)}) copy-start(bf16[8192,128]{1,0:T(8,128)(2,1)} %get-tuple-element.48) | copy-start | bytes 6291460 | tf_op jit(solution)/shard_map/cond
  370.8 73.0 %copy-start.4 = (f32[3584]{0:T(1024)S(1)}, f32[3584]{0:T(1024)}, u32[]{:S(2)}) copy-start(f32[3584]{0:T(1024)} %param.23) | copy-start | bytes 43012
  378.1 70.5 %copy-start.1 = (bf16[3,112,1152]{2,1,0:T(8,128)(2,1)S(1)}, bf16[3,112,1152]{2,1,0:T(8,128)(2,1)}, u32[]{:S(2)}) copy-start(bf16[3,112,1152]{2,1,0:T(8,128)(2,1)} %param.25) | copy-start | bytes 2322436
Sparse Core Ops, SparseCore 0:
  10.0 98.3 all-gather.10
  115.2 76.2 all-gather.6
  194.3 76.5 all-gather.8
  273.4 91.1 all-gather.12
  378.2 65.5 all-reduce.1
where the time goes:
time: 460 us; the launch traced here: 455 us
  waiting for transfers between devices  319 us (69%)
  matrix products  69.5 us (15%)
  other arithmetic  38.9 us (8%)
  between operations  14.4 us (3%)
  local copies, waits for them, and re-layouts  9.21 us (2%)
    all_gather x1, waiting for transfers between devices, on_device(): values_in = lax.all_gather(value_part, 'ctx', axis=0, tiled=True)  79.4 us
    all_gather x1, waiting for transfers between devices, on_device(): keys_in = lax.all_gather(key_part, 'ctx', axis=0, tiled=True)  71.1 us
    psum x1, waiting for transfers between devices, on_device(): lax.psum(section_term.astype(jnp.bfloat16), 'tp').astype(jnp.float32)  65.7 us
    all_gather x1, waiting for transfers between devices, on_device(): lax.all_gather(weight_qkv, 'ctx', axis=0, tiled=True)  56.5 us
    ppermute x1, waiting for transfers between devices, shifted(): return lax.ppermute(value, axis, pairs)  37.8 us
    reduce_sum x2, other arithmetic, update_state(): total_new = jnp.sum(weights, axis=1)  29.1 us
    dot_general x2, matrix products, update_state(): jnp.dot(query_flat, keys_in.T, preferred_element_type=jnp.float32)  28.4 us
    dot_general x2, matrix products, update_state(): jnp.dot(weights.astype(jnp.bfloat16), values_in, preferred_element_type=j...  26.2 us
  transfers between devices with their start and end apart: 6, of which 6 were waited for; matrix products, arithmetic and copies ran while one was open for 20% of the time, Pallas kernels for 0%

commit v1 on v0

--- a/solution.py
+++ b/solution.py
@@ -57,8 +57,6 @@
     merged = (merged + bias_qkv).astype(jnp.bfloat16)
     query_cols = GROUP * HD
     queries = merged[:, :query_cols]
-    key_part = merged[:, query_cols : query_cols + HD]
-    value_part = merged[:, query_cols + HD : query_cols + 2 * HD]
     local_steps = jnp.arange(half_rows, dtype=jnp.int32)
     first_pos = ctx_id * tok_rows + local_steps
     second_q = queries[half_rows:]
@@ -75,8 +73,9 @@
     )
     carried = (empty, empty)
     offset = jnp.int32(0)
-    keys_in = lax.all_gather(key_part, "ctx", axis=0, tiled=True)
-    values_in = lax.all_gather(value_part, "ctx", axis=0, tiled=True)
+    kv_in = lax.all_gather(merged[:, query_cols : query_cols + 2 * HD], "ctx", axis=0, tiled=True)
+    keys_in = kv_in[:, :HD]
+    values_in = kv_in[:, HD:]
     updated = []
     for softmax_state, query_flat, query_pos in (
         (carried[0], first_flat, first_qpos),
@@ -134,7 +133,9 @@
     baseline = jnp.where(
         is_first, jnp.where(is_vision[:, None], b_proj[None, :], text.astype(jnp.float32)), inputs
     )
-    summed = lax.psum(section_term.astype(jnp.bfloat16), "tp").astype(jnp.float32)
+    own_term = section_term.astype(jnp.bfloat16)
+    other_term = lax.ppermute(own_term, "tp", [(0, 1), (1, 0)])
+    summed = own_term.astype(jnp.float32) + other_term.astype(jnp.float32)
     result = (baseline + summed).astype(jnp.bfloat16)
     return result[None]
 

time: 460 us -> 369 us (0.80)
  waiting for transfers between devices: 319 us -> 218 us
  local copies, waits for them, and re-layouts: 9.21 us -> 15.9 us
    all_gather x2 -> x1, waiting for transfers between devices: 151 us -> 78.6 us  [on_device(): lax.all_gather(merged[:, query_cols:query_cols + 2 * HD], 'ctx', axis=0,...]
    psum x1 -> x0, waiting for transfers between devices: 65.7 us -> none  [on_device(): lax.psum(section_term.astype(jnp.bfloat16), 'tp').astype(jnp.float32)]
    ppermute x0 -> x1, waiting for transfers between devices: none -> 42.4 us  [on_device(): other_term = lax.ppermute(own_term, 'tp', [(0, 1), (1, 0)])]
    all_gather x1, waiting for transfers between devices: 7.69 us -> 2.83 us  [on_device(): lax.all_gather(weight_out, 'ctx', axis=1, tiled=True)]
    slice x1 -> x2, local copies, waits for them, and re-layouts: 0.65 us -> 5.43 us  [the longest x1 3.87 us: on_device(): values_in = kv_in[:, HD:]]
  transfers between devices with their start and end apart: 6 -> 5, of which waited for: 6 -> 5; matrix products, arithmetic and copies ran while one was open for 20% -> 27% of each run, Pallas kernels for 0% -> 0%
where the time goes in v1:
time: 369 us; the launch traced here: 362 us
  waiting for transfers between devices  218 us (59%)
  matrix products  69.6 us (19%)
  other arithmetic  39.4 us (11%)
  local copies, waits for them, and re-layouts  15.9 us (4%)
  between operations  14.5 us (4%)
  starting transfers between devices  3.69 us (1%)
    all_gather x1, waiting for transfers between devices, on_device(): lax.all_gather(merged[:, query_cols:query_cols + 2 * HD], 'ctx', axis=0,...  78.6 us
    all_gather x1, waiting for transfers between devices, on_device(): lax.all_gather(weight_qkv, 'ctx', axis=0, tiled=True)  56.5 us
    ppermute x1, waiting for transfers between devices, on_device(): other_term = lax.ppermute(own_term, 'tp', [(0, 1), (1, 0)])  42.4 us
    ppermute x1, waiting for transfers between devices, shifted(): return lax.ppermute(value, axis, pairs)  37.8 us
    reduce_sum x2, other arithmetic, update_state(): total_new = jnp.sum(weights, axis=1)  29.2 us
    dot_general x2, matrix products, update_state(): jnp.dot(query_flat, keys_in.T, preferred_element_type=jnp.float32)  27.8 us
    dot_general x2, matrix products, update_state(): jnp.dot(weights.astype(jnp.bfloat16), values_in, preferred_element_type=j...  26.1 us
  transfers between devices with their start and end apart: 5, of which 5 were waited for; matrix products, arithmetic and copies ran while one was open for 27% of the time, Pallas kernels for 0%

profile of v1, /device:TPU:230, one launch (start us, length us, event | category | flops | bytes accessed | tf_op | source)
XLA Modules:
  0.0 361.5 jit_solution(14345656262956970861)
XLA Ops:
  6.5 0.0 copy-start
  6.5 0.0 all-gather.8.cloned.1.call-start
  6.5 1.1 copy-done
  7.7 0.7 constant_dynamic-slice_fusion.1
  8.4 0.0 all-gather.8.cloned.1.call-update
  8.4 0.0 all-gather.6.cloned.1.call-start
  8.5 3.6 collective-permute-start
  12.1 0.7 dynamic-slice_reduce_fusion.1
  12.8 0.9 dynamic-slice_reduce_fusion
  13.7 37.8 %collective-permute-done = bf16[256,3584]{1,0:T(8,128)(2,1)S(1)} collective-permute-done((bf16[256,3584]{1,0:T(8,128)(2,1)}, bf16[256,3584]{1,0:T(8,128)(2,1)S(1)}, u32[]{:S(2)}, u32[]{:S(2)}) %collective-permute-start) | collective-permute-done | bytes 1835040 | tf_op jit(solution)/shard_map/ppermute | solution.py:16
  51.5 0.4 fusion.31
  52.0 0.0 copy-start.5
  52.0 56.5 %all-gather.8.cloned.1.call-done = bf16[1,3584,1152]{2,1,0:T(8,128)(2,1)} async-done(((bf16[1,112,1152]{2,1,0:T(8,128)(2,1)}), bf16[1,3584,1152]{2,1,0:T(8,128)(2,1)}) %all-gather.8.cloned.1.call-update) | async-done | bytes 8257552 | tf_op jit(solution)/shard_map/all_gather | solution.py:54
  108.5 6.8 %fusion.37 = bf16[256,1152]{1,0:T(8,128)(2,1)} fusion(bf16[1,3584,1152]{2,1,0:T(8,128)(2,1)} %all-gather.8.cloned.1.call-done, bf16[256,3584]{1,0:T(8,128)(2,1)S(1)} %collective-permute-done, f32[3584]{0:T(1024)S(1)} %dynamic-slice_reduce_fusion, f32[256]{0:T(256)S(1)} %add_rsqrt_fusion.1, f32[1152]{0:T(1024)S(1)} %dynamic-slice_reduce_fusion.1), kind=kOutput, calls=%fused_computation.56 | convolution fusion | flops 2118189056 | bytes 10702336 | tf_op jit(solution)/shard_map/dot_general | solution.py:52
  115.2 0.0 copy-done.2
  115.2 1.6 slice.25
  116.8 0.0 all-gather.6.cloned.1.call-update
  116.8 0.0 all-gather.10.cloned.1.call-start
  116.9 1.6 constant_dynamic-slice_fusion
  118.5 0.0 all-gather.10.cloned.1.call-update
  118.5 0.7 broadcast_reduce_fusion.1
  119.9 0.7 broadcast_reduce_fusion
  121.3 0.0 copy-done.5
  121.3 0.1 fusion.48
  121.4 0.1 ge.21
  121.5 78.6 %all-gather.6.cloned.1.call-done = bf16[8192,256]{1,0:T(8,128)(2,1)} async-done(((bf16[256,256]{1,0:T(8,128)(2,1)}), bf16[8192,256]{1,0:T(8,128)(2,1)}) %all-gather.6.cloned.1.call-update) | async-done | bytes 4194320 | tf_op jit(solution)/shard_map/all_gather | solution.py:76
  200.1 3.9 %fusion.49 = (bf16[8192,128]{1,0:T(8,128)(2,1)S(1)}, bf16[8192,128]{1,0:T(8,128)(2,1)}) fusion(bf16[8192,256]{1,0:T(8,128)(2,1)} %all-gather.6.cloned.1.call-done), kind=kLoop, calls=%fused_computation.79 | loop fusion | bytes 8388608 | tf_op jit(solution)/shard_map/slice | solution.py:78
  203.9 0.1 broadcast_in_dim.104
  204.0 43.0 %conditional.3 = (f32[896]{0:T(1024)S(1)}, f32[896,128]{1,0:T(8,128)S(1)}) conditional(s32[]{:T(128)} %convert_element_type.60, () %tuple.37, (s32[128,7]{1,0:T(8,128)S(1)}, bf16[256,1152]{1,0:T(8,128)(2,1)}, bf16[8192,128]{1,0:T(8,128)(2,1)}, bf16[8192,128]{1,0:T(8,128)(2,1)S(1)}) %tuple.38), branch_computations={%region_3.4_spmd, %region_4.7_spmd} | conditional | flops 3875535872 | bytes 93919760 | solution.py:92
  204.0 0.2 le.30
  204.2 1.0 slice.15
  205.2 0.2 reshape.63
  205.4 14.0 %fusion = (f32[896]{0:T(1024)S(1)}, f32[896,8192]{1,0:T(8,128)}) fusion(s32[896]{0:T(1024)S(1)} %le.30, bf16[896,128]{1,0:T(8,128)(2,1)S(1)} %reshape.63, bf16[8192,128]{1,0:T(8,128)(2,1)} %get-tuple-element.49), kind=kOutput, calls=%fused_computation.4 | convolution fusion | flops 1908407424 | bytes 31693824 | tf_op jit(solution)/shard_map/cond/branch_1_fun/dot_general | solution.py:22
  219.4 13.1 %fusion.3 = f32[896,128]{1,0:T(8,128)S(1)} fusion(bf16[8192,128]{1,0:T(8,128)(2,1)S(1)} %get-tuple-element.50, f32[896,8192]{1,0:T(8,128)} %get-tuple-element.92, f32[896]{0:T(1024)S(1)} %broadcast_maximum_fusion, s32[896]{0:T(1024)S(1)} %le.30), kind=kOutput, calls=%fused_computation.7 | convolution fusion | flops 1923088384 | bytes 31923200 | tf_op jit(solution)/shard_map/cond/branch_1_fun/dot_general | solution.py:28
  232.5 14.4 %fusion.2 = f32[896]{0:T(1024)S(1)} fusion(f32[896,8192]{1,0:T(8,128)} %get-tuple-element.92, f32[896]{0:T(1024)S(1)} %broadcast_maximum_fusion, s32[896]{0:T(1024)S(1)} %le.30), kind=kLoop, calls=%fused_computation.6 | loop fusion | flops 44039296 | bytes 29370880 | tf_op jit(solution)/shard_map/cond/branch_1_fun/reduce_sum | solution.py:27
  247.0 0.2 divide_convert_fusion.1
  247.2 0.2 reshape.67
  247.4 0.1 broadcast_in_dim.105
  247.5 0.0 copy-start.6
  247.5 43.3 %conditional.4 = (f32[896]{0:T(1024)S(1)}, f32[896,128]{1,0:T(8,128)S(1)}) conditional(s32[]{:T(128)} %convert_element_type.64, () %tuple.39, (s32[128,7]{1,0:T(8,128)S(1)}, bf16[256,1152]{1,0:T(8,128)(2,1)}, bf16[8192,128]{1,0:T(8,128)(2,1)}, bf16[8192,128]{1,0:T(8,128)(2,1)S(1)}) %tuple.40), branch_computations={%region_8.9_spmd, %region_9.12_spmd} | conditional | flops 3875535872 | bytes 93919760 | solution.py:92
  247.7 0.2 le.38
  247.9 1.0 slice.16
  248.9 0.2 reshape.64
  249.1 13.8 %fusion.8 = (f32[896]{0:T(1024)S(1)}, f32[896,8192]{1,0:T(8,128)}) fusion(s32[896]{0:T(1024)S(1)} %le.38, bf16[896,128]{1,0:T(8,128)(2,1)S(1)} %reshape.64, bf16[8192,128]{1,0:T(8,128)(2,1)} %get-tuple-element.53), kind=kOutput, calls=%fused_computation.15 | convolution fusion | flops 1908407424 | bytes 31693824 | tf_op jit(solution)/shard_map/cond/branch_1_fun/dot_general | solution.py:22
  263.0 13.1 %fusion.11 = f32[896,128]{1,0:T(8,128)S(1)} fusion(bf16[8192,128]{1,0:T(8,128)(2,1)S(1)} %get-tuple-element.54, f32[896,8192]{1,0:T(8,128)} %get-tuple-element.94, f32[896]{0:T(1024)S(1)} %broadcast_maximum_fusion.1, s32[896]{0:T(1024)S(1)} %le.38), kind=kOutput, calls=%fused_computation.18 | convolution fusion | flops 1923088384 | bytes 31923200 | tf_op jit(solution)/shard_map/cond/branch_1_fun/dot_general | solution.py:28
  276.0 14.7 %fusion.10 = f32[896]{0:T(1024)S(1)} fusion(f32[896,8192]{1,0:T(8,128)} %get-tuple-element.94, f32[896]{0:T(1024)S(1)} %broadcast_maximum_fusion.1, s32[896]{0:T(1024)S(1)} %le.38), kind=kLoop, calls=%fused_computation.17 | loop fusion | flops 44039296 | bytes 29370880 | tf_op jit(solution)/shard_map/cond/branch_1_fun/reduce_sum | solution.py:27
  290.8 0.2 divide_convert_fusion
  291.0 0.2 reshape.68
  291.2 2.8 all-gather.10.cloned.1.call-done
  294.1 0.0 copy-done.3
  294.1 0.0 copy-done.6
  294.1 6.2 %fusion.27 = bf16[256,3584]{1,0:T(8,128)(2,1)} fusion(bf16[1,896,3584]{1,2,0:T(8,128)(2,1)} %all-gather.10.cloned.1.call-done, bf16[128,896]{1,0:T(8,128)(2,1)S(1)} %reshape.68, bf16[128,896]{1,0:T(8,128)(2,1)S(1)} %reshape.67), kind=kOutput, calls=%fused_computation.45 | convolution fusion | flops 1645084672 | bytes 8716288 | tf_op jit(solution)/shard_map/dot_general | solution.py:104
  300.2 7.3 %conditional.5 = (bf16[256,3584]{1,0:T(8,128)(2,1)}) conditional(s32[]{:T(128)} %convert_element_type.59, bf16[256,3584]{1,0:T(8,128)(2,1)} %fusion.27, (pred[256]{0:T(512)(128)(4,1)S(1)}, pred[256,2]{0,1:T(4,128)(4,1)S(1)}, bf16[128,1024]{1,0:T(8,128)(2,1)S(1)}, f32[1024]{0:T(1024)S(1)}, s32[]{:T(128)}, /*index=5*/bf16[512,3584]{1,0:T(8,128)(2,1)}, ...), branch_computations={%region_13.14_spmd, %region_14.17_spmd} | conditional | flops 472585344 | bytes 13264226 | solution.py:132
  300.2 0.1 dynamic-slice
  300.3 0.1 convert_reduce_fusion
  300.4 0.2 multiply_reduce_fusion
  300.7 2.7 fusion.18
  303.4 0.1 fusion.23
  303.5 1.7 gather_fusion
  305.3 2.2 select_select_fusion
  307.5 0.0 collective-permute-start.1
  307.5 42.4 %collective-permute-done.1 = bf16[256,3584]{1,0:T(8,128)(2,1)S(1)} collective-permute-done((bf16[256,3584]{1,0:T(8,128)(2,1)}, bf16[256,3584]{1,0:T(8,128)(2,1)S(1)}, u32[]{:S(2)}, u32[]{:S(2)}) %collective-permute-start.1) | collective-permute-done | bytes 1835040 | tf_op jit(solution)/shard_map/ppermute | solution.py:137
  349.9 5.1 %fusion.41 = bf16[1,256,3584]{2,1,0:T(8,128)(2,1)} fusion(bf16[256,3584]{1,0:T(8,128)(2,1)S(1)} %collective-permute-done.1, bf16[256,3584]{1,0:T(8,128)(2,1)} %get-tuple-element.107, bf16[256,3584]{1,0:T(8,128)(2,1)} %copy-done.2, bf16[256,3584]{1,0:T(8,128)(2,1)} %param.18, f32[3584]{0:T(1024)S(1)} %copy-done.4, pred[256]{0:T(512)(128)(4,1)S(1)} %get-tuple-element.89, ...), kind=kLoop, calls=%fused_computation.57 | loop fusion | flops 8257536 | bytes 9189633 | tf_op jit(solution)/shard_map/broadcast_in_dim | solution.py:140
  355.0 0.0 copy-done.1
  (20 shorter events, 0.1 us)
Async XLA Ops:
  6.5 1.1 copy-start
  6.5 101.9 %all-gather.8.cloned.1.call-start = ((), (), s32[]{:S(2)}) async-start(), calls=%async_computation.1 | async-start | bytes 8515584 | tf_op jit(solution)/shard_map/all_gather | solution.py:54
  8.4 191.7 %all-gather.6.cloned.1.call-start = ((), (), s32[]{:S(2)}) async-start(), calls=%async_computation | async-start | bytes 4325376 | tf_op jit(solution)/shard_map/all_gather | solution.py:76
  8.5 43.1 %collective-permute-start = (bf16[256,3584]{1,0:T(8,128)(2,1)}, bf16[256,3584]{1,0:T(8,128)(2,1)S(1)}, u32[]{:S(2)}, u32[]{:S(2)}) collective-permute-start(bf16[256,3584]{1,0:T(8,128)(2,1)} %bitcast.20), channel_id=1, source_target_pairs={{0,64},{64,128},{128,192},{1,65},{65,129},{129,193},{2,66},{66,130... | collective-permute-start | bytes 5505032 | tf_op jit(solution)/shard_map/ppermute | solution.py:16
  51.5 63.7 %copy-start.2 = (bf16[256,3584]{1,0:T(8,128)(2,1)}, bf16[256,3584]{1,0:T(8,128)(2,1)S(1)}, u32[]{:S(2)}) copy-start(bf16[256,3584]{1,0:T(8,128)(2,1)S(1)} %collective-permute-done) | copy-start | bytes 5505028
  52.0 69.4 %copy-start.5 = (s32[2]{0:T(128)S(1)}, s32[2]{0:T(128)}, u32[]{:S(2)}) copy-start(s32[2]{0:T(128)} %param.20) | copy-start | bytes 28
  116.8 177.2 %all-gather.10.cloned.1.call-start = ((), (), s32[]{:S(2)}) async-start(), calls=%async_computation.2 | async-start | bytes 6623232 | tf_op jit(solution)/shard_map/all_gather | solution.py:106
  247.5 46.6 %copy-start.3 = (bf16[128,1024]{1,0:T(8,128)(2,1)S(1)}, bf16[128,1024]{1,0:T(8,128)(2,1)}, u32[]{:S(2)}) copy-start(bf16[128,1024]{1,0:T(8,128)(2,1)} %param.19) | copy-start | bytes 786436
  247.5 46.6 %copy-start.6 = (f32[1024]{0:T(1024)S(1)}, f32[1024]{0:T(1024)}, u32[]{:S(2)}) copy-start(f32[1024]{0:T(1024)} %param.21) | copy-start | bytes 12292
  300.2 49.7 %copy-start.4 = (f32[3584]{0:T(1024)S(1)}, f32[3584]{0:T(1024)}, u32[]{:S(2)}) copy-start(f32[3584]{0:T(1024)} %param.23) | copy-start | bytes 43012
  307.5 47.5 %copy-start.1 = (bf16[3,112,1152]{2,1,0:T(8,128)(2,1)S(1)}, bf16[3,112,1152]{2,1,0:T(8,128)(2,1)}, u32[]{:S(2)}) copy-start(bf16[3,112,1152]{2,1,0:T(8,128)(2,1)} %param.25) | copy-start | bytes 2322436
  307.5 42.4 %collective-permute-start.1 = (bf16[256,3584]{1,0:T(8,128)(2,1)}, bf16[256,3584]{1,0:T(8,128)(2,1)S(1)}, u32[]{:S(2)}, u32[]{:S(2)}) collective-permute-start(bf16[256,3584]{1,0:T(8,128)(2,1)} %get-tuple-element.107), channel_id=1, source_target_pairs={{0,1},{1,0},{2,3},{3,2},{4,5},{5,4},{6,7},{7,6},{8,9},{9,8},{10,11... | collective-permute-start | bytes 5505032 | tf_op jit(solution)/shard_map/ppermute | solution.py:137
Sparse Core Ops, SparseCore 0:
  10.0 98.3 all-gather.7
  116.9 83.0 all-gather.5
  202.8 91.2 all-gather.9

commit v2 on v1

v2 whole, which is shorter than its diff:
```python
import jax
import jax.numpy as jnp
from jax import lax
from jax.experimental import pallas as pl
from jax.experimental.pallas import tpu as pltpu
from jax.sharding import PartitionSpec as P

HD = 128
GROUP = 7
FRAME = 64
KEY_BLOCK = 512


def attention_kernel(ctx_ref, q_ref, k_ref, v_ref, o_ref, m_sc, l_sc, acc_sc):
    step_id = pl.program_id(0)
    rows = q_ref.shape[0]
    q_start = ctx_ref[0] * rows
    last_step = (q_start + rows - 1) // KEY_BLOCK

    @pl.when(step_id == 0)
    def _():
        m_sc[...] = jnp.full(m_sc.shape, -1e30, jnp.float32)
        l_sc[...] = jnp.zeros(l_sc.shape, jnp.float32)
        acc_sc[...] = jnp.zeros(acc_sc.shape, jnp.float32)

    def update(masked):
        keys = k_ref[...]
        values = v_ref[...]
        if masked:
            query_pos = q_start + lax.broadcasted_iota(jnp.int32, (rows, KEY_BLOCK), 0)
            key_pos = step_id * KEY_BLOCK + lax.broadcasted_iota(jnp.int32, (rows, KEY_BLOCK), 1)
            allowed = key_pos <= query_pos
        for head in range(GROUP):
            cols = slice(head * HD, (head + 1) * HD)
            scores = lax.dot_general(
                q_ref[:, cols], keys, (((1,), (1,)), ((), ())), preferred_element_type=jnp.float32
            ) * HD ** (-0.5)
            if masked:
                scores = jnp.where(allowed, scores, -1e30)
            peak_old = m_sc[head]
            peak_new = jnp.maximum(peak_old, jnp.max(scores, axis=1, keepdims=True))
            rescale = jnp.exp(peak_old - peak_new)
            weights = jnp.exp(scores - peak_new)
            if masked:
                weights = jnp.where(allowed, weights, 0.0)
            l_sc[head] = rescale * l_sc[head] + jnp.sum(weights, axis=1, keepdims=True)
            acc_sc[:, cols] = rescale * acc_sc[:, cols] + jnp.dot(
                weights.astype(jnp.bfloat16), values, preferred_element_type=jnp.float32
            )
            m_sc[head] = peak_new

    @pl.when((step_id + 1) * KEY_BLOCK - 1 <= q_start)
    def _():
        update(False)

    @pl.when(jnp.logical_and((step_id + 1) * KEY_BLOCK - 1 > q_start, step_id <= last_step))
    def _():
        update(True)

    @pl.when(step_id == pl.num_programs(0) - 1)
    def _():
        for head in range(GROUP):
            cols = slice(head * HD, (head + 1) * HD)
            o_ref[:, cols] = (acc_sc[:, cols] / l_sc[head]).astype(o_ref.dtype)


def causal_attention(ctx_id, merged, kv_in):
    rows = merged.shape[0]
    tokens = kv_in.shape[0]
    width = GROUP * HD

    def kv_map(col):
        def index(step_id, ctx_ref):
            last_step = (ctx_ref[0] * rows + rows - 1) // KEY_BLOCK
            return (jnp.minimum(step_id, last_step), col)
        return index

    flops = 4 * rows * GROUP * tokens * HD
    return pl.pallas_call(
        attention_kernel,
        out_shape=jax.ShapeDtypeStruct((rows, width), jnp.bfloat16),
        grid_spec=pltpu.PrefetchScalarGridSpec(
            num_scalar_prefetch=1,
            grid=(tokens // KEY_BLOCK,),
            in_specs=[
                pl.BlockSpec((rows, width), lambda step_id, ctx_ref: (0, 0)),
                pl.BlockSpec((KEY_BLOCK, HD), kv_map(0)),
                pl.BlockSpec((KEY_BLOCK, HD), kv_map(1)),
            ],
            out_specs=pl.BlockSpec((rows, width), lambda step_id, ctx_ref: (0, 0)),
            scratch_shapes=[
                pltpu.VMEM((GROUP, rows, 1), jnp.float32),
                pltpu.VMEM((GROUP, rows, 1), jnp.float32),
                pltpu.VMEM((rows, width), jnp.float32),
            ],
        ),
        compiler_params=pltpu.CompilerParams(dimension_semantics=("arbitrary",)),
        cost_estimate=pl.CostEstimate(
            flops=flops, transcendentals=rows * GROUP * tokens, bytes_accessed=kv_in.size * 2 + 4 * rows * width
        ),
    )(jnp.reshape(ctx_id, (1,)).astype(jnp.int32), merged, kv_in, kv_in)


def shifted(value, axis, by):
    devices = lax.axis_size(axis)
    pairs = [(i, i + by) for i in range(devices) if 0 <= i + by < devices]
    return lax.ppermute(value, axis, pairs)


def on_device(held, text, frames, join, ln_gain, w_proj, b_proj, norm_gain, w_qkv, b_qkv, w_out):
    segment_id = lax.axis_index("segment")
    ctx_id = lax.axis_index("ctx")
    tp_id = lax.axis_index("tp")
    hidden_in = shifted(held[0], "segment", 1)
    tok_rows = hidden_in.shape[0]
    layer_id = jnp.maximum(segment_id - 1, 0)
    weight_qkv = lax.dynamic_index_in_dim(w_qkv, layer_id, 0, keepdims=False)
    bias_qkv = lax.dynamic_index_in_dim(b_qkv, layer_id, 0, keepdims=False)
    layer_gain = lax.dynamic_index_in_dim(norm_gain, layer_id, 0, keepdims=False)
    weight_out = lax.dynamic_index_in_dim(w_out, layer_id, 0, keepdims=False)
    qkv_cols = weight_qkv.shape[1]
    packed = jnp.concatenate([weight_qkv, weight_out.T], axis=1)
    gathered = lax.all_gather(packed, "ctx", axis=0, tiled=True)
    weight_qkv_full = gathered[:, :qkv_cols]
    weight_out_cols = gathered[:, qkv_cols:]
    inputs = hidden_in.astype(jnp.float32)
    normed = (
        inputs * lax.rsqrt(jnp.mean(inputs * inputs, axis=1, keepdims=True) + 1e-06) * layer_gain
    ).astype(jnp.bfloat16)
    merged = jnp.dot(normed, weight_qkv_full, preferred_element_type=jnp.float32)
    merged = (merged + bias_qkv).astype(jnp.bfloat16)
    query_cols = GROUP * HD
    kv_in = lax.all_gather(merged[:, query_cols : query_cols + 2 * HD], "ctx", axis=0, tiled=True)
    attended = causal_attention(ctx_id, merged, kv_in)
    partial_model = lax.dot_general(
        attended, weight_out_cols, (((1,), (1,)), ((), ())), preferred_element_type=jnp.float32
    )
    positions = ctx_id * tok_rows + jnp.arange(tok_rows, dtype=jnp.int32)[:, None]
    starts = join[None, :]
    inside = (positions >= starts) & (positions < starts + FRAME)
    frame_base = (jnp.arange(join.shape[0], dtype=jnp.int32) * FRAME)[None, :]
    source = jnp.sum(jnp.where(inside, frame_base + positions - starts, 0), axis=1)
    is_vision = jnp.any(inside, axis=1)

    def vision_term():
        frame_in = frames.astype(jnp.float32)
        center = jnp.mean(frame_in, axis=1, keepdims=True)
        spread = jnp.mean((frame_in - center) * (frame_in - center), axis=1, keepdims=True)
        normed_frames = ((frame_in - center) * lax.rsqrt(spread + 1e-06) * ln_gain).astype(
            jnp.bfloat16
        )
        vis_width = w_proj.shape[0]
        normed_half = lax.dynamic_slice_in_dim(normed_frames, tp_id * vis_width, vis_width, 1)
        projected = jnp.dot(normed_half, w_proj, preferred_element_type=jnp.float32)
        return jnp.where(is_vision[:, None], jnp.take(projected, source, axis=0), 0.0)

    def model_term():
        return partial_model

    is_first = segment_id == 0
    section_term = lax.cond(is_first, vision_term, model_term)
    baseline = jnp.where(
        is_first, jnp.where(is_vision[:, None], b_proj[None, :], text.astype(jnp.float32)), inputs
    )
    own_term = section_term.astype(jnp.bfloat16)
    other_term = lax.ppermute(own_term, "tp", [(0, 1), (1, 0)])
    summed = own_term.astype(jnp.float32) + other_term.astype(jnp.float32)
    result = (baseline + summed).astype(jnp.bfloat16)
    return result[None]


def solution(mesh):
    return jax.shard_map(
        on_device,
        mesh=mesh,
        in_specs=(
            P("segment", "ctx", None),
            P("ctx", None),
            P("ctx", None),
            P("ctx"),
            P(),
            P("tp", None),
            P(),
            P(),
            P(None, "ctx", "tp"),
            P(None, "tp"),
            P(None, "tp", "ctx"),
        ),
        out_specs=P("segment", "ctx", None),
        check_vma=False,
    )
```

time: 369 us -> 349 us (0.946); the launches traced: 362 us -> 348 us
  matrix products: 69.6 us -> 15 us
  Pallas kernels: 0 us -> 54.4 us
  other arithmetic: 39.4 us -> 9.17 us
  waiting for transfers between devices: 218 us -> 246 us
  local copies, waits for them, and re-layouts: 15.9 us -> 6.89 us
    dot_general x6 -> x2, matrix products: 66.9 us -> 12.3 us  [the longest x1 6.31 us: on_device(): lax.dot_general(attended, weight_out_cols, (((1,), (1,)), ((), ())), pref...]
    pallas_call x0 -> x1, Pallas kernels: none -> 54.4 us  [causal_attention(): pl.pallas_call(attention_kernel, out_shape=jax.ShapeDtypeStruct((rows, wi...]
    reduce_sum x2 -> x0, other arithmetic: 29.2 us -> none  [update_state(): total_new = jnp.sum(weights, axis=1)]
    all_gather x2 -> x1, waiting for transfers between devices: 59.3 us -> 81.4 us  [on_device(): gathered = lax.all_gather(packed, 'ctx', axis=0, tiled=True)]
    slice x3 -> x0, local copies, waits for them, and re-layouts: 5.79 us -> none  [the longest x1 3.87 us: on_device(): values_in = kv_in[:, HD:]]
    all_gather x1, waiting for transfers between devices: 78.6 us -> 83.9 us  [on_device(): lax.all_gather(merged[:, query_cols:query_cols + 2 * HD], 'ctx', axis=0,...]
  transfers between devices with their start and end apart: 5 -> 4, of which waited for: 5 -> 4; matrix products, arithmetic and copies ran while one was open for 27% -> 1% of each run, Pallas kernels for 0% -> 0%
where the time goes in v2:
time: 349 us; the launch traced here: 348 us
  waiting for transfers between devices  246 us (70%)
  Pallas kernels  54.4 us (16%)
  matrix products  15 us (4%)
  between operations  13.5 us (4%)
  other arithmetic  9.17 us (3%)
  local copies, waits for them, and re-layouts  6.89 us (2%)
  starting transfers between devices  3.65 us (1%)
    all_gather x1, waiting for transfers between devices, on_device(): lax.all_gather(merged[:, query_cols:query_cols + 2 * HD], 'ctx', axis=0,...  83.9 us
    all_gather x1, waiting for transfers between devices, on_device(): gathered = lax.all_gather(packed, 'ctx', axis=0, tiled=True)  81.4 us
    pallas_call x1, Pallas kernels, causal_attention(): pl.pallas_call(attention_kernel, out_shape=jax.ShapeDtypeStruct((rows, wi...  54.4 us
    ppermute x1, waiting for transfers between devices, on_device(): other_term = lax.ppermute(own_term, 'tp', [(0, 1), (1, 0)])  42.4 us
    ppermute x1, waiting for transfers between devices, shifted(): return lax.ppermute(value, axis, pairs)  37.8 us
  transfers between devices with their start and end apart: 4, of which 4 were waited for; matrix products, arithmetic and copies ran while one was open for 1% of the time, Pallas kernels for 0%

profile of v2, /device:TPU:230, one launch (start us, length us, event | category | flops | bytes accessed | tf_op | source)
XLA Modules:
  0.0 348.2 jit_solution(13123372875211022565)
XLA Ops:
  6.5 0.0 copy-start
  6.5 0.0 all-gather.3.cloned.1.call-start
  6.5 1.1 copy-done
  7.7 1.0 dynamic-slice_bitcast_fusion.1
  8.6 0.8 pad_maximum_fusion
  9.5 0.0 all-gather.3.cloned.1.call-update
  9.5 0.0 all-gather.5.cloned.1.call-start
  9.5 3.6 %collective-permute-start = (bf16[256,3584]{1,0:T(8,128)(2,1)}, bf16[256,3584]{1,0:T(8,128)(2,1)S(1)}, u32[]{:S(2)}, u32[]{:S(2)}) collective-permute-start(bf16[256,3584]{1,0:T(8,128)(2,1)} %bitcast.12), channel_id=1, source_target_pairs={{0,64},{64,128},{128,192},{1,65},{65,129},{129,193},{2,66},{66,130... | collective-permute-start | bytes 5505032 | tf_op jit(solution)/shard_map/ppermute | solution.py:107
  13.1 0.7 dynamic-slice_reduce_fusion.1
  13.9 0.9 dynamic-slice_reduce_fusion
  14.8 37.8 %collective-permute-done = bf16[256,3584]{1,0:T(8,128)(2,1)S(1)} collective-permute-done((bf16[256,3584]{1,0:T(8,128)(2,1)}, bf16[256,3584]{1,0:T(8,128)(2,1)S(1)}, u32[]{:S(2)}, u32[]{:S(2)}) %collective-permute-start) | collective-permute-done | bytes 1835040 | tf_op jit(solution)/shard_map/ppermute | solution.py:107
  52.6 0.0 copy-start.1
  52.6 0.4 fusion.15
  53.0 0.0 copy-start.7
  53.1 81.4 %all-gather.3.cloned.1.call-done = bf16[3584,2048]{1,0:T(8,128)(2,1)} async-done(((bf16[112,2048]{1,0:T(8,128)(2,1)}), bf16[3584,2048]{1,0:T(8,128)(2,1)}) %all-gather.3.cloned.1.call-update) | async-done | bytes 14680080 | tf_op jit(solution)/shard_map/all_gather | solution.py:123
  134.4 5.9 %fusion.21.q_ref = bf16[256,1152]{1,0:T(8,128)(2,1)S(1)} fusion(bf16[3584,2048]{1,0:T(8,128)(2,1)} %all-gather.3.cloned.1.call-done, bf16[256,3584]{1,0:T(8,128)(2,1)S(1)} %collective-permute-done, f32[3584]{0:T(1024)S(1)} %dynamic-slice_reduce_fusion, f32[256]{0:T(256)S(1)} %add_rsqrt_fusion.1, f32[1152]{0:T(1024)S(1)} %dynamic-slice_reduce_fusion.1), kind=kOutput, calls=%fused_computation.34 | convolution fusion | flops 2118189056 | bytes 10702336 | tf_op jit(solution)/shard_map/dot_general | solution.py:130
  140.4 0.0 copy-done.1
  140.4 0.0 copy-start.3
  140.4 0.7 slice.15
  141.1 0.0 all-gather.5.cloned.1.call-update
  141.2 0.0 copy-done.7
  141.2 0.1 fusion.28
  141.3 0.1 ge.21
  141.3 83.9 %all-gather.5.cloned.1.call-done.k_ref.v_ref = bf16[8192,256]{1,0:T(8,128)(2,1)} async-done(((bf16[256,256]{1,0:T(8,128)(2,1)}), bf16[8192,256]{1,0:T(8,128)(2,1)}) %all-gather.5.cloned.1.call-update) | async-done | bytes 4194320 | tf_op jit(solution)/shard_map/all_gather | solution.py:133
  225.2 0.0 copy-done.3
  225.2 0.0 copy-start.2
  225.2 0.0 copy-start.8
  225.2 54.4 %shard_map.112 = bf16[256,896]{1,0:T(8,128)(2,1)} custom-call(s32[1]{0:T(128)} %bitcast.1.ctx_ref, bf16[256,1152]{1,0:T(8,128)(2,1)} %copy-done.3, bf16[8192,256]{1,0:T(8,128)(2,1)} %all-gather.5.cloned.1.call-done.k_ref.v_ref, bf16[8192,256]{1,0:T(8,128)(2,1)} %all-gather.5.cloned.1.call-done.k_ref.v_ref), custom_call_target="tpu_custom_call" | custom-call | flops 7516192768 | bytes 5111808 | tf_op jit(solution)/shard_map/pallas_call | solution.py:79
  279.7 0.0 copy-done.2
  279.7 0.0 copy-done.8
  279.7 6.3 %fusion.11 = bf16[256,3584]{1,0:T(8,128)(2,1)} fusion(bf16[256,896]{1,0:T(8,128)(2,1)} %shard_map.112, bf16[3584,2048]{1,0:T(8,128)(2,1)} %all-gather.3.cloned.1.call-done), kind=kOutput, calls=%fused_computation.23 | convolution fusion | flops 1644167168 | bytes 8716288 | tf_op jit(solution)/shard_map/dot_general | solution.py:135
  286.0 0.0 copy-start.4
  286.0 7.8 %conditional.1 = (bf16[256,3584]{1,0:T(8,128)(2,1)}) conditional(s32[]{:T(128)} %convert_element_type.41, bf16[256,3584]{1,0:T(8,128)(2,1)} %fusion.11, (pred[256]{0:T(512)(128)(4,1)S(1)}, pred[256,2]{0,1:T(4,128)(4,1)S(1)}, bf16[128,1024]{1,0:T(8,128)(2,1)S(1)}, f32[1024]{0:T(1024)S(1)}, s32[]{:T(128)}, /*index=5*/bf16[512,3584]{1,0:T(8,128)(2,1)}, ...), branch_computations={%region_3.4_spmd, %region_4.7_spmd} | conditional | flops 472585344 | bytes 13272474 | solution.py:161
  286.0 0.1 dynamic-slice
  286.1 0.1 convert_reduce_fusion
  286.2 0.2 multiply_reduce_fusion
  286.4 2.7 fusion.2
  289.2 0.1 fusion.7
  289.3 0.0 copy-start.5
  289.3 0.6 copy-done.5
  289.8 0.0 copy-start.6
  289.8 1.7 gather_fusion
  291.6 0.0 copy-done.6
  291.6 2.2 select_select_fusion
  293.8 0.0 collective-permute-start.1
  293.8 42.4 %collective-permute-done.1 = bf16[256,3584]{1,0:T(8,128)(2,1)S(1)} collective-permute-done((bf16[256,3584]{1,0:T(8,128)(2,1)}, bf16[256,3584]{1,0:T(8,128)(2,1)S(1)}, u32[]{:S(2)}, u32[]{:S(2)}) %collective-permute-start.1) | collective-permute-done | bytes 1835040 | tf_op jit(solution)/shard_map/ppermute | solution.py:166
  336.2 0.0 copy-done.4
  336.2 5.1 %fusion.25 = bf16[1,256,3584]{2,1,0:T(8,128)(2,1)} fusion(bf16[256,3584]{1,0:T(8,128)(2,1)S(1)} %collective-permute-done.1, bf16[256,3584]{1,0:T(8,128)(2,1)} %get-tuple-element.57, bf16[256,3584]{1,0:T(8,128)(2,1)} %copy-done.1, bf16[256,3584]{1,0:T(8,128)(2,1)} %param.14, f32[3584]{0:T(1024)S(1)} %copy-done.4, pred[256]{0:T(512)(128)(4,1)S(1)} %get-tuple-element.53, ...), kind=kLoop, calls=%fused_computation.35 | loop fusion | flops 8257536 | bytes 9189633 | tf_op jit(solution)/shard_map/broadcast_in_dim | solution.py:169
  (12 shorter events, 0.1 us)
Async XLA Ops:
  6.5 1.1 copy-start
  6.5 127.9 %all-gather.3.cloned.1.call-start = ((), (), s32[]{:S(2)}) async-start(), calls=%async_computation | async-start | bytes 15138816 | tf_op jit(solution)/shard_map/all_gather | solution.py:123
  9.5 215.8 %all-gather.5.cloned.1.call-start = ((), (), s32[]{:S(2)}) async-start(), calls=%async_computation.1 | async-start | bytes 4325376 | tf_op jit(solution)/shard_map/all_gather | solution.py:133
  9.5 43.1 %collective-permute-start = (bf16[256,3584]{1,0:T(8,128)(2,1)}, bf16[256,3584]{1,0:T(8,128)(2,1)S(1)}, u32[]{:S(2)}, u32[]{:S(2)}) collective-permute-start(bf16[256,3584]{1,0:T(8,128)(2,1)} %bitcast.12), channel_id=1, source_target_pairs={{0,64},{64,128},{128,192},{1,65},{65,129},{129,193},{2,66},{66,130... | collective-permute-start | bytes 5505032 | tf_op jit(solution)/shard_map/ppermute | solution.py:107
  52.6 87.8 %copy-start.1 = (bf16[256,3584]{1,0:T(8,128)(2,1)}, bf16[256,3584]{1,0:T(8,128)(2,1)S(1)}, u32[]{:S(2)}) copy-start(bf16[256,3584]{1,0:T(8,128)(2,1)S(1)} %collective-permute-done) | copy-start | bytes 5505028
  53.0 88.1 %copy-start.7 = (s32[2]{0:T(128)S(1)}, s32[2]{0:T(128)}, u32[]{:S(2)}) copy-start(s32[2]{0:T(128)} %param.16) | copy-start | bytes 28
  140.4 84.9 %copy-start.3 = (bf16[256,1152]{1,0:T(8,128)(2,1)}, bf16[256,1152]{1,0:T(8,128)(2,1)S(1)}, u32[]{:S(2)}) copy-start(bf16[256,1152]{1,0:T(8,128)(2,1)S(1)} %fusion.21.q_ref) | copy-start | bytes 1769476
  225.2 54.4 %copy-start.2 = (bf16[128,1024]{1,0:T(8,128)(2,1)S(1)}, bf16[128,1024]{1,0:T(8,128)(2,1)}, u32[]{:S(2)}) copy-start(bf16[128,1024]{1,0:T(8,128)(2,1)} %param.15) | copy-start | bytes 786436
  225.2 54.4 %copy-start.8 = (f32[1024]{0:T(1024)S(1)}, f32[1024]{0:T(1024)}, u32[]{:S(2)}) copy-start(f32[1024]{0:T(1024)} %param.17) | copy-start | bytes 12292
  286.0 50.2 %copy-start.4 = (f32[3584]{0:T(1024)S(1)}, f32[3584]{0:T(1024)}, u32[]{:S(2)}) copy-start(f32[3584]{0:T(1024)} %param.19) | copy-start | bytes 43012
  289.3 0.6 copy-start.5
  289.8 1.7 copy-start.6
  293.8 42.4 %collective-permute-start.1 = (bf16[256,3584]{1,0:T(8,128)(2,1)}, bf16[256,3584]{1,0:T(8,128)(2,1)S(1)}, u32[]{:S(2)}, u32[]{:S(2)}) collective-permute-start(bf16[256,3584]{1,0:T(8,128)(2,1)} %get-tuple-element.57), channel_id=1, source_target_pairs={{0,1},{1,0},{2,3},{3,2},{4,5},{5,4},{6,7},{7,6},{8,9},{9,8},{10,11... | collective-permute-start | bytes 5505032 | tf_op jit(solution)/shard_map/ppermute | solution.py:166
Sparse Core Ops, SparseCore 0:
  10.1 124.2 all-gather.2
  141.3 83.9 all-gather.4

commit v3 on v2

--- a/solution.py
+++ b/solution.py
@@ -8,13 +8,14 @@
 HD = 128
 GROUP = 7
 FRAME = 64
-KEY_BLOCK = 512
+KEY_BLOCK = 2048
+CHUNKS = 1
 
 
 def attention_kernel(ctx_ref, q_ref, k_ref, v_ref, o_ref, m_sc, l_sc, acc_sc):
     step_id = pl.program_id(0)
     rows = q_ref.shape[0]
-    q_start = ctx_ref[0] * rows
+    q_start = ctx_ref[0]
     last_step = (q_start + rows - 1) // KEY_BLOCK
 
     @pl.when(step_id == 0)
@@ -64,14 +65,13 @@
             o_ref[:, cols] = (acc_sc[:, cols] / l_sc[head]).astype(o_ref.dtype)
 
 
-def causal_attention(ctx_id, merged, kv_in):
-    rows = merged.shape[0]
+def causal_attention(q_start, merged, kv_in, chunk, rows):
     tokens = kv_in.shape[0]
     width = GROUP * HD
 
     def kv_map(col):
-        def index(step_id, ctx_ref):
-            last_step = (ctx_ref[0] * rows + rows - 1) // KEY_BLOCK
+        def index(step_id, start_ref):
+            last_step = (start_ref[0] + rows - 1) // KEY_BLOCK
             return (jnp.minimum(step_id, last_step), col)
         return index
 
@@ -83,11 +83,11 @@
             num_scalar_prefetch=1,
             grid=(tokens // KEY_BLOCK,),
             in_specs=[
-                pl.BlockSpec((rows, width), lambda step_id, ctx_ref: (0, 0)),
+                pl.BlockSpec((rows, width), lambda step_id, start_ref: (chunk, 0)),
                 pl.BlockSpec((KEY_BLOCK, HD), kv_map(0)),
                 pl.BlockSpec((KEY_BLOCK, HD), kv_map(1)),
             ],
-            out_specs=pl.BlockSpec((rows, width), lambda step_id, ctx_ref: (0, 0)),
+            out_specs=pl.BlockSpec((rows, width), lambda step_id, start_ref: (0, 0)),
             scratch_shapes=[
                 pltpu.VMEM((GROUP, rows, 1), jnp.float32),
                 pltpu.VMEM((GROUP, rows, 1), jnp.float32),
@@ -98,7 +98,7 @@
         cost_estimate=pl.CostEstimate(
             flops=flops, transcendentals=rows * GROUP * tokens, bytes_accessed=kv_in.size * 2 + 4 * rows * width
         ),
-    )(jnp.reshape(ctx_id, (1,)).astype(jnp.int32), merged, kv_in, kv_in)
+    )(jnp.reshape(q_start, (1,)).astype(jnp.int32), merged, kv_in, kv_in)
 
 
 def shifted(value, axis, by):
@@ -131,10 +131,6 @@
     merged = (merged + bias_qkv).astype(jnp.bfloat16)
     query_cols = GROUP * HD
     kv_in = lax.all_gather(merged[:, query_cols : query_cols + 2 * HD], "ctx", axis=0, tiled=True)
-    attended = causal_attention(ctx_id, merged, kv_in)
-    partial_model = lax.dot_general(
-        attended, weight_out_cols, (((1,), (1,)), ((), ())), preferred_element_type=jnp.float32
-    )
     positions = ctx_id * tok_rows + jnp.arange(tok_rows, dtype=jnp.int32)[:, None]
     starts = join[None, :]
     inside = (positions >= starts) & (positions < starts + FRAME)
@@ -154,18 +150,36 @@
         projected = jnp.dot(normed_half, w_proj, preferred_element_type=jnp.float32)
         return jnp.where(is_vision[:, None], jnp.take(projected, source, axis=0), 0.0)
 
-    def model_term():
-        return partial_model
-
     is_first = segment_id == 0
-    section_term = lax.cond(is_first, vision_term, model_term)
-    baseline = jnp.where(
-        is_first, jnp.where(is_vision[:, None], b_proj[None, :], text.astype(jnp.float32)), inputs
-    )
-    own_term = section_term.astype(jnp.bfloat16)
-    other_term = lax.ppermute(own_term, "tp", [(0, 1), (1, 0)])
-    summed = own_term.astype(jnp.float32) + other_term.astype(jnp.float32)
-    result = (baseline + summed).astype(jnp.bfloat16)
+    vision_rows = lax.cond(is_first, vision_term, lambda: jnp.zeros((tok_rows, w_proj.shape[1]), jnp.float32))
+    chunk_rows = tok_rows // CHUNKS
+    pieces = []
+    own_term = None
+    for chunk in range(CHUNKS):
+        rows_here = slice(chunk * chunk_rows, (chunk + 1) * chunk_rows)
+        if own_term is not None:
+            own_term, merged = lax.optimization_barrier((own_term, merged))
+            pieces[-1] = (pieces[-1][0], own_term)
+        attended = causal_attention(
+            ctx_id * tok_rows + chunk * chunk_rows, merged, kv_in, chunk, chunk_rows
+        )
+        partial_model = lax.dot_general(
+            attended, weight_out_cols, (((1,), (1,)), ((), ())), preferred_element_type=jnp.float32
+        )
+        section_term = jnp.where(is_first, vision_rows[rows_here], partial_model)
+        baseline = jnp.where(
+            is_first,
+            jnp.where(is_vision[rows_here, None], b_proj[None, :], text[rows_here].astype(jnp.float32)),
+            inputs[rows_here],
+        )
+        own_term = section_term.astype(jnp.bfloat16)
+        pieces.append((baseline, own_term))
+    results = []
+    for baseline, own_term in pieces:
+        other_term = lax.ppermute(own_term, "tp", [(0, 1), (1, 0)])
+        summed = own_term.astype(jnp.float32) + other_term.astype(jnp.float32)
+        results.append((baseline + summed).astype(jnp.bfloat16))
+    result = jnp.concatenate(results, axis=0)
     return result[None]
 
 

time: 349 us -> 316 us (0.905)
  Pallas kernels: 54.4 us -> 32.5 us
  waiting for transfers between devices: 246 us -> 238 us
    pallas_call x1, Pallas kernels: 54.4 us -> 32.5 us  [causal_attention(): pl.pallas_call(attention_kernel, out_shape=jax.ShapeDtypeStruct((rows, wi...]
    all_gather x1, waiting for transfers between devices: 83.9 us -> 76.6 us  [on_device(): lax.all_gather(merged[:, query_cols:query_cols + 2 * HD], 'ctx', axis=0,...]
  transfers between devices with their start and end apart: 4 -> 4, of which waited for: 4 -> 4; matrix products, arithmetic and copies ran while one was open for 1% -> 3% of each run, Pallas kernels for 0% -> 0%
where the time goes in v3:
time: 316 us
  waiting for transfers between devices  238 us (75%)
  Pallas kernels  32.5 us (10%)
  matrix products  14.4 us (5%)
  between operations  13.5 us (4%)
  local copies, waits for them, and re-layouts  7.08 us (2%)
  other arithmetic  6.43 us (2%)
  starting transfers between devices  3.73 us (1%)
    all_gather x1, waiting for transfers between devices, on_device(): gathered = lax.all_gather(packed, 'ctx', axis=0, tiled=True)  81.3 us
    all_gather x1, waiting for transfers between devices, on_device(): lax.all_gather(merged[:, query_cols:query_cols + 2 * HD], 'ctx', axis=0,...  76.6 us
    ppermute x1, waiting for transfers between devices, on_device(): other_term = lax.ppermute(own_term, 'tp', [(0, 1), (1, 0)])  42.2 us
    ppermute x1, waiting for transfers between devices, shifted(): return lax.ppermute(value, axis, pairs)  37.8 us
    pallas_call x1, Pallas kernels, causal_attention(): pl.pallas_call(attention_kernel, out_shape=jax.ShapeDtypeStruct((rows, wi...  32.5 us
  transfers between devices with their start and end apart: 4, of which 4 were waited for; matrix products, arithmetic and copies ran while one was open for 3% of the time, Pallas kernels for 0%

profile of v3, /device:TPU:230, one launch (start us, length us, event | category | flops | bytes accessed | tf_op | source)
XLA Modules:
  0.0 315.7 jit_solution(10814771005667270096)
XLA Ops:
  6.5 0.0 copy-start
  6.5 0.0 all-gather.3.cloned.1.call-start
  6.5 1.1 copy-done
  7.7 1.0 dynamic-slice_bitcast_fusion.1
  8.6 0.8 pad_maximum_fusion
  9.5 0.0 all-gather.3.cloned.1.call-update
  9.5 0.0 all-gather.5.cloned.1.call-start
  9.5 3.6 %collective-permute-start = (bf16[256,3584]{1,0:T(8,128)(2,1)}, bf16[256,3584]{1,0:T(8,128)(2,1)S(1)}, u32[]{:S(2)}, u32[]{:S(2)}) collective-permute-start(bf16[256,3584]{1,0:T(8,128)(2,1)} %bitcast.12), channel_id=1, source_target_pairs={{0,64},{64,128},{128,192},{1,65},{65,129},{129,193},{2,66},{66,130... | collective-permute-start | bytes 5505032 | tf_op jit(solution)/shard_map/ppermute | solution.py:107
  13.1 0.7 dynamic-slice_reduce_fusion.1
  13.9 0.9 dynamic-slice_reduce_fusion
  14.8 37.8 %collective-permute-done = bf16[256,3584]{1,0:T(8,128)(2,1)S(1)} collective-permute-done((bf16[256,3584]{1,0:T(8,128)(2,1)}, bf16[256,3584]{1,0:T(8,128)(2,1)S(1)}, u32[]{:S(2)}, u32[]{:S(2)}) %collective-permute-start) | collective-permute-done | bytes 1835040 | tf_op jit(solution)/shard_map/ppermute | solution.py:107
  52.6 0.0 copy-start.1
  52.6 0.4 fusion.21
  53.0 0.0 copy-start.7
  53.1 0.0 copy-start.4
  53.1 0.0 copy-start.8
  53.1 81.3 %all-gather.3.cloned.1.call-done = bf16[3584,2048]{1,0:T(8,128)(2,1)} async-done(((bf16[112,2048]{1,0:T(8,128)(2,1)}), bf16[3584,2048]{1,0:T(8,128)(2,1)}) %all-gather.3.cloned.1.call-update) | async-done | bytes 14680080 | tf_op jit(solution)/shard_map/all_gather | solution.py:123
  134.4 5.9 %fusion.27.q_ref = bf16[256,1152]{1,0:T(8,128)(2,1)S(1)} fusion(bf16[3584,2048]{1,0:T(8,128)(2,1)} %all-gather.3.cloned.1.call-done, bf16[256,3584]{1,0:T(8,128)(2,1)S(1)} %collective-permute-done, f32[3584]{0:T(1024)S(1)} %dynamic-slice_reduce_fusion, f32[256]{0:T(256)S(1)} %add_rsqrt_fusion.1, f32[1152]{0:T(1024)S(1)} %dynamic-slice_reduce_fusion.1), kind=kOutput, calls=%fused_computation.36 | convolution fusion | flops 2118189056 | bytes 10702336 | tf_op jit(solution)/shard_map/dot_general | solution.py:130
  140.4 0.0 copy-done.1
  140.4 0.0 copy-start.5
  140.4 0.8 copy-done.5
  141.2 0.7 slice.15
  141.9 0.0 all-gather.5.cloned.1.call-update
  141.9 0.0 copy-done.7
  141.9 0.1 fusion.34
  142.0 0.1 ge.21
  142.1 0.0 copy-done.4
  142.1 0.0 copy-done.8
  142.1 7.3 %conditional.1 = (bf16[256,3584]{1,0:T(8,128)(2,1)}) conditional(s32[]{:T(128)} %convert_element_type.35, () %tuple.11, (pred[256]{0:T(512)(128)(4,1)S(1)}, pred[256,2]{0,1:T(4,128)(4,1)S(1)}, bf16[128,1024]{1,0:T(8,128)(2,1)S(1)}, f32[1024]{0:T(1024)S(1)}, s32[]{:T(128)}, /*index=5*/bf16[512,3584]{1,0:T(8,128)(2,1)}, s32[]{:T(128)}, s32[2]{0:T(128)S(1)}, ...), branch_computations={%region_2.3_spmd, %region_3.6_spmd} | conditional | flops 472585344 | bytes 13264226 | solution.py:154
  142.1 0.1 dynamic-slice
  142.2 0.1 convert_reduce_fusion
  142.3 0.2 multiply_reduce_fusion
  142.5 2.7 fusion.2
  145.3 0.1 fusion.7
  145.4 1.7 gather_fusion
  147.1 2.2 select_select_fusion
  149.4 76.6 %all-gather.5.cloned.1.call-done.k_ref.v_ref = bf16[8192,256]{1,0:T(8,128)(2,1)} async-done(((bf16[256,256]{1,0:T(8,128)(2,1)}), bf16[8192,256]{1,0:T(8,128)(2,1)}) %all-gather.5.cloned.1.call-update) | async-done | bytes 4194320 | tf_op jit(solution)/shard_map/all_gather | solution.py:133
  226.0 32.5 %shard_map.112 = bf16[256,896]{1,0:T(8,128)(2,1)} custom-call(s32[1]{0:T(128)} %bitcast.1.ctx_ref, bf16[256,1152]{1,0:T(8,128)(2,1)} %copy-done.5, bf16[8192,256]{1,0:T(8,128)(2,1)} %all-gather.5.cloned.1.call-done.k_ref.v_ref, bf16[8192,256]{1,0:T(8,128)(2,1)} %all-gather.5.cloned.1.call-done.k_ref.v_ref), custom_call_target="tpu_custom_call" | custom-call | flops 7516192768 | bytes 5111808 | tf_op jit(solution)/shard_map/pallas_call | solution.py:79
  258.5 0.0 copy-start.2
  258.5 0.0 copy-start.3
  258.5 0.0 copy-start.6
  258.5 5.7 %fusion.16 = bf16[256,3584]{1,0:T(8,128)(2,1)S(1)} fusion(bf16[256,3584]{1,0:T(8,128)(2,1)} %get-tuple-element.50, bf16[256,896]{1,0:T(8,128)(2,1)} %shard_map.112, bf16[3584,2048]{1,0:T(8,128)(2,1)} %all-gather.3.cloned.1.call-done, pred[]{:T(512)S(6)} %eq.3), kind=kOutput, calls=%fused_computation.29 | convolution fusion | flops 1645084672 | bytes 10551297 | tf_op jit(solution)/shard_map/dot_general | solution.py:166
  264.2 0.1 collective-permute-start.1
  264.3 42.2 %collective-permute-done.1 = bf16[256,3584]{1,0:T(8,128)(2,1)S(1)} collective-permute-done((bf16[256,3584]{1,0:T(8,128)(2,1)S(1)}, bf16[256,3584]{1,0:T(8,128)(2,1)S(1)}, u32[]{:S(2)}, u32[]{:S(2)}) %collective-permute-start.1) | collective-permute-done | bytes 1835040 | tf_op jit(solution)/shard_map/ppermute | solution.py:179
  306.5 0.0 copy-done.2
  306.5 0.0 copy-done.3
  306.5 0.0 copy-done.6
  306.5 2.4 fusion.31
  (12 shorter events, 0.1 us)
Async XLA Ops:
  6.5 1.1 copy-start
  6.5 127.9 %all-gather.3.cloned.1.call-start = ((), (), s32[]{:S(2)}) async-start(), calls=%async_computation | async-start | bytes 15138816 | tf_op jit(solution)/shard_map/all_gather | solution.py:123
  9.5 216.5 %all-gather.5.cloned.1.call-start = ((), (), s32[]{:S(2)}) async-start(), calls=%async_computation.1 | async-start | bytes 4325376 | tf_op jit(solution)/shard_map/all_gather | solution.py:133
  9.5 43.1 %collective-permute-start = (bf16[256,3584]{1,0:T(8,128)(2,1)}, bf16[256,3584]{1,0:T(8,128)(2,1)S(1)}, u32[]{:S(2)}, u32[]{:S(2)}) collective-permute-start(bf16[256,3584]{1,0:T(8,128)(2,1)} %bitcast.12), channel_id=1, source_target_pairs={{0,64},{64,128},{128,192},{1,65},{65,129},{129,193},{2,66},{66,130... | collective-permute-start | bytes 5505032 | tf_op jit(solution)/shard_map/ppermute | solution.py:107
  52.6 87.8 %copy-start.1 = (bf16[256,3584]{1,0:T(8,128)(2,1)}, bf16[256,3584]{1,0:T(8,128)(2,1)S(1)}, u32[]{:S(2)}) copy-start(bf16[256,3584]{1,0:T(8,128)(2,1)S(1)} %collective-permute-done) | copy-start | bytes 5505028
  53.0 88.9 %copy-start.7 = (s32[2]{0:T(128)S(1)}, s32[2]{0:T(128)}, u32[]{:S(2)}) copy-start(s32[2]{0:T(128)} %param.16) | copy-start | bytes 28
  53.1 89.0 %copy-start.4 = (bf16[128,1024]{1,0:T(8,128)(2,1)S(1)}, bf16[128,1024]{1,0:T(8,128)(2,1)}, u32[]{:S(2)}) copy-start(bf16[128,1024]{1,0:T(8,128)(2,1)} %param.15) | copy-start | bytes 786436
  53.1 89.0 %copy-start.8 = (f32[1024]{0:T(1024)S(1)}, f32[1024]{0:T(1024)}, u32[]{:S(2)}) copy-start(f32[1024]{0:T(1024)} %param.17) | copy-start | bytes 12292
  140.4 0.8 copy-start.5
  258.5 48.0 %copy-start.2 = (bf16[256,3584]{1,0:T(8,128)(2,1)S(1)}, bf16[256,3584]{1,0:T(8,128)(2,1)}, u32[]{:S(2)}) copy-start(bf16[256,3584]{1,0:T(8,128)(2,1)} %copy-done.1) | copy-start | bytes 5505028
  258.5 48.0 %copy-start.3 = (bf16[256,3584]{1,0:T(8,128)(2,1)S(1)}, bf16[256,3584]{1,0:T(8,128)(2,1)}, u32[]{:S(2)}) copy-start(bf16[256,3584]{1,0:T(8,128)(2,1)} %param.14) | copy-start | bytes 5505028
  258.5 48.0 %copy-start.6 = (f32[3584]{0:T(1024)S(1)}, f32[3584]{0:T(1024)}, u32[]{:S(2)}) copy-start(f32[3584]{0:T(1024)} %param.19) | copy-start | bytes 43012
  264.2 42.3 %collective-permute-start.1 = (bf16[256,3584]{1,0:T(8,128)(2,1)S(1)}, bf16[256,3584]{1,0:T(8,128)(2,1)S(1)}, u32[]{:S(2)}, u32[]{:S(2)}) collective-permute-start(bf16[256,3584]{1,0:T(8,128)(2,1)S(1)} %fusion.16), channel_id=1, source_target_pairs={{0,1},{1,0},{2,3},{3,2},{4,5},{5,4},{6,7},{7,6},{8,9},{9,8},{10,11... | collective-permute-start | bytes 5505032 | tf_op jit(solution)/shard_map/ppermute | solution.py:179
Sparse Core Ops, SparseCore 0:
  10.1 124.2 all-gather.2
  142.0 83.9 all-gather.4
